TPU v7x, 512 devices: a whole 4x4x16 slice. The times are simulated.
512 devices in a mesh: chol: 32 (over y, z_hi, x), pair: 16 (over z_lo, core).
Axes of the slice: x: 4, y: 4, z: 16 (z_hi: 2, z_lo: 8; z = z_hi * 8 + z_lo), core: 2. Of those that a mesh axis runs over, the one named last changes fastest.
Arguments:
- rotated: float32 [16384, 32768], P('chol', 'pair'), may hold values from -0.03125 to 0.03125
- green: float32 [1024, 32768], P('chol', 'pair'), may hold values from -6 to 6
- aux_field: float32 [1024, 16384], P('pair', 'chol'), may hold values from -6 to 6
Outputs:
- shifted: float32 [1024, 16384], P('pair', 'chol')
All inputs are finite; a program needn't handle non-finite values.
Results may differ from a plain program's by a relative error of at most 0.000056.
Values sent between devices are 32-bit elements; how exact they have to be, the bound alone decides.
No kernel may reach another device: no remote copies, remote signals or barrier semaphores. Data moves between devices by JAX's collectives and lax.ppermute only.
A program may use at most 64 MiB of HBM per device.

v0:
```python
import jax
import jax.numpy as jnp
from jax import lax
from jax.sharding import PartitionSpec as P

bias_cap = 1.5


def contract(rows, rotated):
    return lax.dot_general(
        rows,
        rotated,
        (((1,), (1,)), ((), ())),
        precision=lax.Precision.HIGHEST,
        preferred_element_type=jnp.float32,
    )


def body(rotated, green, aux_field):
    own_rows = aux_field.shape[0]
    gathered = contract(lax.all_gather(green, "chol", axis=0, tiled=True), rotated)
    total = lax.psum(gathered, "pair")
    share = lax.dynamic_slice_in_dim(total, lax.axis_index("pair") * own_rows, own_rows, 0)
    capped = jnp.clip(share, -bias_cap, bias_cap)
    return aux_field - capped


def solution(mesh):
    placed = (P("chol", "pair"), P("chol", "pair"), P("pair", "chol"))
    return jax.shard_map(
        body, mesh=mesh, in_specs=placed, out_specs=P("pair", "chol"), check_vma=False
    )
```

profile of v0, /device:TPU:14, one launch (start us, length us, event | category | flops | bytes accessed | tf_op | source)
XLA Modules:
  0.0 492.2 jit_solution(11579798569337451576)
XLA Ops:
  6.5 0.0 all-gather.2.cloned.1.call-start
  6.5 0.7 all-gather.2.cloned.1.call-update
  7.3 0.0 copy-start
  7.3 0.0 all-reduce.2.cloned.1.call-start
  7.3 252.7 %all-gather.2.cloned.1.call-done = f32[1024,2048]{1,0:T(8,128)} async-done(((f32[32,2048]{1,0:T(8,128)}), f32[1024,2048]{1,0:T(8,128)}) %all-gather.2.cloned.1.call-update) | async-done | bytes 8388624 | tf_op jit(solution)/shard_map/all_gather | solution.py:21
  260.0 17.1 %fusion = f32[1024,512]{1,0:T(8,128)} fusion(f32[1024,2048]{1,0:T(8,128)} %all-gather.2.cloned.1.call-done, f32[512,2048]{1,0:T(8,128)} %param.3), kind=kOutput, calls=%fused_computation.1 | convolution fusion | flops 12884901888 | bytes 14680064 | tf_op jit(solution)/shard_map/dot_general | solution.py:10
  277.1 0.0 all-reduce.2.cloned.1.call-update
  277.1 206.6 %all-reduce.2.cloned.1.call-done = f32[1024,512]{1,0:T(8,128)} async-done(((f32[1024,512]{1,0:T(8,128)}), f32[1024,512]{1,0:T(8,128)}) %all-reduce.2.cloned.1.call-update) | async-done | bytes 2097168 | tf_op jit(solution)/shard_map/psum | solution.py:22
  483.7 0.0 copy-done
  483.7 1.6 clamp_subtract_fusion
Async XLA Ops:
  6.5 253.5 %all-gather.2.cloned.1.call-start = ((), (), s32[]{:S(2)}) async-start(), calls=%async_computation | async-start | bytes 8650752 | tf_op jit(solution)/shard_map/all_gather | solution.py:21
  7.3 476.5 %copy-start = (f32[64,512]{1,0:T(8,128)S(1)}, f32[64,512]{1,0:T(8,128)}, u32[]{:S(2)}) copy-start(f32[64,512]{1,0:T(8,128)} %param.5) | copy-start | bytes 393220
  7.3 476.5 %all-reduce.2.cloned.1.call-start = ((), (), s32[]{:S(2)}) async-start(), calls=%async_computation.1 | async-start | bytes 4194304 | tf_op jit(solution)/shard_map/psum | solution.py:22
Sparse Core Ops, SparseCore 0:
  11.7 248.2 all-gather.1
  277.2 206.4 all-reduce.1
where the time goes:
time: 492 us
  waiting for transfers between devices  460 us (93%)
  matrix products  17.1 us (3%)
  between operations  13.4 us (3%)
    all_gather x1, waiting for transfers between devices, body(): lax.all_gather(green, 'chol', axis=0, tiled=True)  253 us
    psum x1, waiting for transfers between devices, body(): total = lax.psum(gathered, 'pair')  207 us
    dot_general x1, matrix products, contract(): lax.dot_general(rows, rotated, (((1,), (1,)), ((), ())), precision=lax.Pr...  17.1 us
  transfers between devices with their start and end apart: 2, of which 2 were waited for; matrix products, arithmetic and copies ran while one was open for 0% of the time, Pallas kernels for 0%

commit v1 on v0

--- a/solution.py
+++ b/solution.py
@@ -19,7 +19,7 @@
 def body(rotated, green, aux_field):
     own_rows = aux_field.shape[0]
     gathered = contract(lax.all_gather(green, "chol", axis=0, tiled=True), rotated)
-    total = lax.psum(gathered, "pair")
+    total = jnp.sum(lax.all_gather(gathered, "pair"), axis=0)
     share = lax.dynamic_slice_in_dim(total, lax.axis_index("pair") * own_rows, own_rows, 0)
     capped = jnp.clip(share, -bias_cap, bias_cap)
     return aux_field - capped

time: 492 us -> 662 us (1.35)
  the two profiles are of different devices: /device:TPU:14 before, /device:TPU:2 now
where the time goes in v1:
time: 662 us; the launch traced here: 661 us
  waiting for transfers between devices  617 us (93%)
  matrix products  17.1 us (3%)
  other arithmetic  13.4 us (2%)
  between operations  13.4 us (2%)
    all_gather x1, waiting for transfers between devices, body(): total = jnp.sum(lax.all_gather(gathered, 'pair'), axis=0)  363 us
    all_gather x1, waiting for transfers between devices, body(): lax.all_gather(green, 'chol', axis=0, tiled=True)  253 us
    dot_general x1, matrix products, contract(): lax.dot_general(rows, rotated, (((1,), (1,)), ((), ())), precision=lax.Pr...  17.1 us
  transfers between devices with their start and end apart: 2, of which 2 were waited for; matrix products, arithmetic and copies ran while one was open for 0% of the time, Pallas kernels for 0%

profile of v1, /device:TPU:2, one launch (start us, length us, event | category | flops | bytes accessed | tf_op | source)
XLA Modules:
  0.0 661.4 jit_solution(6305187999962749164)
XLA Ops:
  6.5 0.0 all-gather.4.cloned.1.call-start
  6.5 0.7 all-gather.4.cloned.1.call-update
  7.3 0.0 all-gather.6.cloned.1.call-start
  7.3 253.3 %all-gather.4.cloned.1.call-done = f32[1024,2048]{1,0:T(8,128)} async-done(((f32[32,2048]{1,0:T(8,128)}), f32[1024,2048]{1,0:T(8,128)}) %all-gather.4.cloned.1.call-update) | async-done | bytes 8388624 | tf_op jit(solution)/shard_map/all_gather | solution.py:21
  260.6 17.1 %fusion = f32[1024,512]{1,0:T(8,128)} fusion(f32[1024,2048]{1,0:T(8,128)} %all-gather.4.cloned.1.call-done, f32[512,2048]{1,0:T(8,128)} %param.3), kind=kOutput, calls=%fused_computation.1 | convolution fusion | flops 12884901888 | bytes 14680064 | tf_op jit(solution)/shard_map/dot_general | solution.py:10
  277.7 0.0 all-gather.6.cloned.1.call-update
  277.7 363.5 %all-gather.6.cloned.1.call-done = f32[16384,512]{1,0:T(8,128)} async-done(((f32[1024,512]{1,0:T(8,128)}), f32[16384,512]{1,0:T(8,128)}) %all-gather.6.cloned.1.call-update) | async-done | bytes 33554448 | tf_op jit(solution)/shard_map/all_gather | solution.py:22
  641.2 0.0 copy-start
  641.2 12.7 %reduce_sum.9 = f32[1024,512]{1,0:T(8,128)S(1)} reduce(f32[16,1024,512]{2,1,0:T(8,128)} %bitcast.3, f32[]{:T(128)} %constant.1.clone.1), dimensions={0}, to_apply=%region_0.0 | reduce | flops 7864320 | bytes 35651588 | tf_op jit(solution)/shard_map/reduce_sum | solution.py:22
  653.9 0.0 copy-done
  653.9 0.7 clamp_subtract_fusion
Async XLA Ops:
  6.5 254.0 %all-gather.4.cloned.1.call-start = ((), (), s32[]{:S(2)}) async-start(), calls=%async_computation | async-start | bytes 8650752 | tf_op jit(solution)/shard_map/all_gather | solution.py:21
  7.3 633.9 %all-gather.6.cloned.1.call-start = ((), (), s32[]{:S(2)}) async-start(), calls=%async_computation.1 | async-start | bytes 35651584 | tf_op jit(solution)/shard_map/all_gather | solution.py:22
  641.2 12.7 %copy-start = (f32[64,512]{1,0:T(8,128)S(1)}, f32[64,512]{1,0:T(8,128)}, u32[]{:S(2)}) copy-start(f32[64,512]{1,0:T(8,128)} %param.5) | copy-start | bytes 393220
Sparse Core Ops, SparseCore 0:
  11.7 248.7 all-gather.3
  277.8 363.2 all-gather.5
